TPU v7x, 512 devices: a whole 4x8x8 slice. The times are simulated.
512 devices in a mesh: section: 8 (over z), kv: 64 (over x, y, core).
Axes of the slice: x: 4, y: 8, z: 8, core: 2. Of those that a mesh axis runs over, the one named last changes fastest.
Arguments:
- held: bfloat16 [8, 128, 8192], P('section', None, 'kv'), may hold values from -6 to 6
- fresh: bfloat16 [1, 128, 8192], P(None, None, 'kv'), may hold values from -6 to 6
- block_starts: int32 [8], replicated, may hold values from 12288 to 24576
- fresh_starts: int32 [1], replicated, may hold values from 12288 to 24576
- norm_gain: float32 [8, 8192], P('section'), may hold values from 0.25 to 1.75
- w_qkv: bfloat16 [8, 8192, 5120], P('section', None, 'kv'), may hold values from -0.0625 to 0.0625
- w_out: bfloat16 [8, 4096, 8192], P('section', None, 'kv'), may hold values from -12 to 12
- cache_keys: bfloat16 [8, 24576, 512], P('section', 'kv'), may hold values from -400 to 400
- cache_values: bfloat16 [8, 24576, 512], P('section', 'kv'), may hold values from -6 to 6
- cache_lengths: int32 [8, 64], P('section', 'kv'), may hold values from 96 to 384, as said below
Outputs:
- produced: bfloat16 [8, 2, 128, 8192], P('section', None, None, 'kv')
Inputs may be any that keep to these rules, and one draw needn't show every extreme that they name: `cache_lengths`: each section has one block filled to 384.
All inputs are finite; a program needn't handle non-finite values.
Results may differ from a plain program's by a relative error of at most 0.017.
The roundings to bfloat16 on the way count: a program that leaves them out, or rounds other values in their place, can miss the bound.
Values may be sent and summed in bfloat16 or wider, within the bound.
No kernel may reach another device: no remote copies, remote signals or barrier semaphores. Data moves between devices by JAX's collectives and lax.ppermute only.
A program may use at most 128 MiB of HBM per device.

v0:
```python
import jax
import jax.numpy as jnp
from jax import lax
from jax.sharding import PartitionSpec as P

HD = 128
HEADS_Q = 32
KV_HEADS = 4


def passed_along(block, axis, distance):
    devices = range(lax.axis_size(axis))
    route = [(i - distance, i) for i in devices if i - distance in devices]
    return lax.ppermute(block, axis, route)


def block_partial(query, key_rows, value_rows, valid):
    row_count = query.shape[0]
    head_count = query.shape[1]
    head_width = query.shape[2]
    group_count = key_rows.shape[1]
    group_size = head_count // group_count
    shaped = jnp.transpose(
        query.reshape(row_count, group_count, group_size, head_width), (1, 0, 2, 3)
    )
    key_major = jnp.transpose(key_rows, (1, 0, 2))
    value_major = jnp.transpose(value_rows, (1, 0, 2))
    allowed = valid[:, None, :]

    def one_group(packed):
        group_query, group_keys, group_values = packed
        scores = jnp.einsum(
            "tgd,id->tgi", group_query, group_keys, preferred_element_type=jnp.float32
        ) * head_width ** (-0.5)
        row_max = jnp.max(jnp.where(allowed, scores, -1e30), axis=2)
        expo = jnp.where(allowed, jnp.exp(scores - row_max[..., None]), 0.0)
        row_sum = jnp.sum(expo, axis=2)
        weights = expo.astype(jnp.bfloat16)
        weighted = jnp.einsum(
            "tgi,id->tgd", weights, group_values, preferred_element_type=jnp.float32
        )
        return (row_max, row_sum, weighted)

    maxima, totals, sums = lax.map(one_group, (shaped, key_major, value_major))
    maxima = jnp.transpose(maxima, (1, 0, 2)).reshape(row_count, head_count)
    totals = jnp.transpose(totals, (1, 0, 2)).reshape(row_count, head_count)
    sums = jnp.transpose(sums, (1, 0, 2, 3)).reshape(row_count, head_count * head_width)
    return (maxima, totals, sums)


def combine_two(left_part, right_part):
    head_count = left_part[0].shape[1]
    row_count = left_part[0].shape[0]
    overall = jnp.maximum(left_part[0], right_part[0])
    left_factor = jnp.exp(left_part[0] - overall)
    right_factor = jnp.exp(right_part[0] - overall)
    total = left_part[1] * left_factor + right_part[1] * right_factor
    left_sum = left_part[2].reshape(row_count, head_count, -1) * left_factor[..., None]
    right_sum = right_part[2].reshape(row_count, head_count, -1) * right_factor[..., None]
    return (overall, total, (left_sum + right_sum).reshape(row_count, -1))


def merge_stack(maxima, totals, sums):
    count = maxima.shape[0]
    row_count = maxima.shape[1]
    head_count = maxima.shape[2]
    overall = jnp.max(maxima, axis=0)
    factor = jnp.exp(maxima - overall)
    total = jnp.sum(totals * factor, axis=0)
    summed = jnp.sum(sums.reshape(count, row_count, head_count, -1) * factor[..., None], axis=0)
    return (summed / total[..., None]).reshape(row_count, -1).astype(jnp.bfloat16)


def on_device(
    held,
    fresh,
    block_starts,
    fresh_starts,
    norm_gain,
    w_qkv,
    w_out,
    cache_keys,
    cache_values,
    cache_lengths,
):
    kv_index = lax.axis_index("kv")
    section_index = lax.axis_index("section")
    tick_count = fresh.shape[0] + 1
    row_count = held.shape[1]
    slot_count = cache_keys.shape[1]
    key_rows = cache_keys[0].reshape(slot_count, KV_HEADS, HD)
    value_rows = cache_values[0].reshape(slot_count, KV_HEADS, HD)
    filled = cache_lengths[0, 0]
    gain = norm_gain[0]
    weight_in = w_qkv[0]
    weight_out = w_out[0]
    slot_ids = jnp.arange(slot_count, dtype=jnp.int32)
    positions = kv_index * slot_count + slot_ids
    row_ids = jnp.arange(row_count, dtype=jnp.int32)
    causal = row_ids[None, :] <= row_ids[:, None]
    current = held[0]
    results = []
    for tick_index in range(tick_count):
        if tick_index > 0:
            passed = passed_along(current, "section", 1)
            current = jnp.where(section_index == 0, fresh[tick_index - 1], passed)
        anchor = section_index - tick_index
        start = jnp.where(
            anchor >= 0,
            block_starts[jnp.maximum(anchor, 0)],
            fresh_starts[jnp.clip(-anchor - 1, 0, tick_count - 2)],
        )
        gathered = lax.all_gather(current, "kv", axis=1, tiled=True)
        wide = gathered.astype(jnp.float32)
        normed = (
            wide * lax.rsqrt(jnp.mean(wide * wide, axis=1, keepdims=True) + 1e-05) * gain
        ).astype(jnp.bfloat16)
        local_cols = jnp.dot(normed, weight_in, preferred_element_type=jnp.float32).astype(
            jnp.bfloat16
        )
        united = lax.all_gather(local_cols, "kv", axis=1, tiled=True)
        query = united[:, : HEADS_Q * HD].reshape(row_count, HEADS_Q, HD)
        new_keys = united[:, HEADS_Q * HD : (HEADS_Q + KV_HEADS) * HD].reshape(
            row_count, KV_HEADS, HD
        )
        new_values = united[:, (HEADS_Q + KV_HEADS) * HD :].reshape(row_count, KV_HEADS, HD)
        usable = (slot_ids < filled) & (positions < start)
        valid = jnp.broadcast_to(usable[None, :], (row_count, slot_count))
        partial_value = block_partial(query, key_rows, value_rows, valid)

        def with_own(parts):
            return combine_two(parts, block_partial(query, new_keys, new_values, causal))

        def without_own(parts):
            return parts

        partial_value = lax.cond(kv_index == 0, with_own, without_own, partial_value)
        received = (
            lax.all_to_all(partial_value[0][None], "kv", split_axis=1, concat_axis=0, tiled=True),
            lax.all_to_all(partial_value[1][None], "kv", split_axis=1, concat_axis=0, tiled=True),
            lax.all_to_all(partial_value[2][None], "kv", split_axis=1, concat_axis=0, tiled=True),
        )
        attended = merge_stack(received[0], received[1], received[2])
        branch = jnp.dot(
            lax.all_gather(attended, "kv", axis=0, tiled=True),
            weight_out,
            preferred_element_type=jnp.float32,
        )
        current = (current.astype(jnp.float32) + branch).astype(jnp.bfloat16)
        results.append(current)
    return jnp.stack(results, 0)[None]


def solution(mesh):
    in_specs = (
        P("section", None, "kv"),
        P(None, None, "kv"),
        P(),
        P(),
        P("section", None),
        P("section", None, "kv"),
        P("section", None, "kv"),
        P("section", "kv", None),
        P("section", "kv", None),
        P("section", "kv"),
    )
    out_specs = P("section", None, None, "kv")
    return jax.shard_map(
        on_device, mesh=mesh, in_specs=in_specs, out_specs=out_specs, check_vma=False
    )
```

profile of v0, /device:TPU:1, one launch (start us, length us, event | category | flops | bytes accessed | tf_op | source)
XLA Modules:
  0.0 792.7 jit_solution(17048475888363732458)
XLA Ops:
  7.3 86.4 %all-gather.16.cloned.1.call-done = bf16[1,128,8192]{2,1,0:T(8,128)(2,1)} async-done(((bf16[1,128,128]{2,1,0:T(8,128)(2,1)}), bf16[1,128,8192]{2,1,0:T(8,128)(2,1)}) %all-gather.16.cloned.1.call-update) | async-done | bytes 2097168 | tf_op jit(solution)/shard_map/all_gather | solution.py:113
  93.7 2.2 fusion.77
  96.0 1.6 fusion.97
  103.6 75.6 %all-gather.10.cloned.1.call-done = bf16[128,5120]{0,1:T(8,128)(2,1)} async-done(((bf16[128,80]{0,1:T(8,128)(2,1)}), bf16[128,5120]{0,1:T(8,128)(2,1)}) %all-gather.10.cloned.1.call-update) | async-done | bytes 1310736 | tf_op jit(solution)/shard_map/all_gather | solution.py:121
  182.1 13.5 %while.58 = (s32[]{:T(128)}, f32[4,128,8]{1,2,0:T(8,128)S(1)}, f32[4,128,8]{1,2,0:T(8,128)S(1)}, f32[4,128,8,128]{3,1,2,0:T(8,128)S(1)}, bf16[4,128,8,128]{3,1,2...) while((s32[]{:T(128)}, f32[4,128,8]{1,2,0:T(8,128)S(1)}, ...), condition=%wide.region_4.5_spmd.clone, body=%wide.region_1.4_spmd.clone.sunk | while | flops 204863488 | bytes 5737833 | solution.py:44
  182.1 1.5 select_reduce_fusion.8
  184.1 1.3 fusion.142
  185.5 1.5 select_reduce_fusion.8
  187.5 1.3 fusion.142
  188.9 1.5 select_reduce_fusion.8
  190.9 1.3 fusion.142
  192.2 1.5 select_reduce_fusion.8
  195.6 12.1 %conditional.2 = (f32[128,32]{0,1:T(8,128)S(1)}, f32[128,32]{0,1:T(8,128)S(1)}, f32[128,4096]{1,0:T(8,128)}) conditional(s32[]{:T(128)} %convert_element_type.53, (f32[128,4,8,128]{3,0,2,1:T(8,128)S(1)}, f32[128,32]{0,1:T(8,128)S(1)}, f32[128,32]{0,1:T(8,128)S(1)}) %tuple.192, (bf16[128,4096]{0,1:T(8,128)(2,1)}, bf16[128,5120]{0,1:T(8,128)(2,1)}, ...), branch_computations={%region_5.6_spmd, %region_6.11_spmd} | conditional | flops 69883904 | bytes 51759524 | solution.py:137
  196.8 3.0 copy.131
  208.4 25.7 %all-to-all-start.2 = ((f32[1,128,32]{2,0,1:T(1,128)}), f32[1,128,32]{2,0,1:T(1,128)S(1)}, u32[]{:S(2)}, u32[]{:S(2)}) async-start(f32[1,128,32]{2,0,1:T(1,128)} %bitcast.73), calls=%async_computation.2 | async-start | bytes 131072 | tf_op jit(solution)/shard_map/all_to_all | solution.py:140
  234.8 9.2 %all-to-all-done.2 = f32[1,128,32]{2,0,1:T(1,128)S(1)} async-done(((f32[1,128,32]{2,0,1:T(1,128)}), f32[1,128,32]{2,0,1:T(1,128)S(1)}, u32[]{:S(2)}, u32[]{:S(2)}) %all-to-all-start.2) | async-done | bytes 16416 | tf_op jit(solution)/shard_map/all_to_all | solution.py:140
  244.0 4.4 all-to-all-start.1
  248.4 5.3 broadcast_in_dim.169
  253.8 4.5 all-to-all-done.1
  258.3 5.9 all-to-all-start
  265.9 49.5 %all-to-all-done = f32[1,128,4096]{2,0,1:T(1,128)S(1)} async-done(((f32[1,128,4096]{2,0,1:T(1,128)}), f32[1,128,4096]{2,0,1:T(1,128)S(1)}, u32[]{:S(2)}, u32[]{:S(2)}) %all-to-all-start) | async-done | bytes 2097184 | tf_op jit(solution)/shard_map/all_to_all | solution.py:141
  316.0 4.3 multiply_reduce_fusion.1
  321.1 79.2 %all-gather.18.cloned.1.call-done = bf16[64,2,4096]{2,1,0:T(2,128)(2,1)} async-done(((bf16[1,2,4096]{2,1,0:T(2,128)(2,1)}), bf16[64,2,4096]{2,1,0:T(2,128)(2,1)}) %all-gather.18.cloned.1.call-update) | async-done | bytes 1048592 | tf_op jit(solution)/shard_map/all_gather | solution.py:145
  400.3 1.5 reshape.190
  402.2 3.3 collective-permute-start
  407.3 78.1 %all-gather.12.cloned.1.call-done = bf16[128,8192]{1,0:T(8,128)(2,1)} async-done(((bf16[128,128]{1,0:T(8,128)(2,1)}), bf16[128,8192]{1,0:T(8,128)(2,1)}) %all-gather.12.cloned.1.call-update) | async-done | bytes 2097168 | tf_op jit(solution)/shard_map/all_gather | solution.py:113
  485.5 2.2 fusion.74
  487.7 1.6 fusion.92
  489.4 81.6 %all-gather.14.cloned.1.call-done = bf16[128,5120]{0,1:T(8,128)(2,1)} async-done(((bf16[128,80]{0,1:T(8,128)(2,1)}), bf16[128,5120]{0,1:T(8,128)(2,1)}) %all-gather.14.cloned.1.call-update) | async-done | bytes 1310736 | tf_op jit(solution)/shard_map/all_gather | solution.py:121
  573.9 13.5 %while.59 = (s32[]{:T(128)}, f32[4,128,8]{1,2,0:T(8,128)S(1)}, f32[4,128,8]{1,2,0:T(8,128)S(1)}, f32[4,128,8,128]{3,1,2,0:T(8,128)S(1)}, bf16[4,128,8,128]{3,1,2...) while((s32[]{:T(128)}, f32[4,128,8]{1,2,0:T(8,128)S(1)}, ...), condition=%wide.region_18.19_spmd.clone, body=%wide.region_15.18_spmd.clone.sunk | while | flops 204863488 | bytes 5737833 | solution.py:44
  573.9 1.5 select_reduce_fusion.9
  577.3 1.5 select_reduce_fusion.9
  579.3 1.3 fusion.146
  580.6 1.5 select_reduce_fusion.9
  584.0 1.5 select_reduce_fusion.9
  586.0 1.3 fusion.146
  587.4 4.4 conditional.3
  588.6 3.0 copy.132
  592.5 24.2 %all-to-all-start.5 = ((f32[1,128,32]{2,0,1:T(1,128)}), f32[1,128,32]{2,0,1:T(1,128)S(1)}, u32[]{:S(2)}, u32[]{:S(2)}) async-start(f32[1,128,32]{2,0,1:T(1,128)} %bitcast.95), calls=%async_computation.5 | async-start | bytes 131072 | tf_op jit(solution)/shard_map/all_to_all | solution.py:140
  617.4 9.2 %all-to-all-done.5 = f32[1,128,32]{2,0,1:T(1,128)S(1)} async-done(((f32[1,128,32]{2,0,1:T(1,128)}), f32[1,128,32]{2,0,1:T(1,128)S(1)}, u32[]{:S(2)}, u32[]{:S(2)}) %all-to-all-start.5) | async-done | bytes 16416 | tf_op jit(solution)/shard_map/all_to_all | solution.py:140
  626.6 4.4 all-to-all-start.4
  631.0 5.3 broadcast_in_dim.172
  636.3 4.5 all-to-all-done.4
  640.9 5.9 all-to-all-start.3
  647.1 50.9 %all-to-all-done.3 = f32[1,128,4096]{2,0,1:T(1,128)S(1)} async-done(((f32[1,128,4096]{2,0,1:T(1,128)}), f32[1,128,4096]{2,0,1:T(1,128)S(1)}, u32[]{:S(2)}, u32[]{:S(2)}) %all-to-all-start.3) | async-done | bytes 2097184 | tf_op jit(solution)/shard_map/all_to_all | solution.py:141
  698.6 4.3 multiply_reduce_fusion
  703.6 79.3 %all-gather.20.cloned.1.call-done = bf16[64,2,4096]{2,1,0:T(2,128)(2,1)} async-done(((bf16[1,2,4096]{2,1,0:T(2,128)(2,1)}), bf16[64,2,4096]{2,1,0:T(2,128)(2,1)}) %all-gather.20.cloned.1.call-update) | async-done | bytes 1048592 | tf_op jit(solution)/shard_map/all_gather | solution.py:145
  782.9 1.5 reshape.192
  (109 shorter events, 31.6 us)
Async XLA Ops:
  6.5 89.4 %copy-start = (bf16[1,8192,80]{1,2,0:T(8,128)(2,1)S(1)}, bf16[1,8192,80]{1,2,0:T(8,128)(2,1)}, u32[]{:S(2)}) copy-start(bf16[1,8192,80]{1,2,0:T(8,128)(2,1)} %param.27) | copy-start | bytes 3932164
  6.5 89.4 %copy-start.27 = (f32[1,8192]{1,0:T(1,128)S(1)}, f32[1,8192]{1,0:T(1,128)}, u32[]{:S(2)}) copy-start(f32[1,8192]{1,0:T(1,128)} %param.26) | copy-start | bytes 98308
  6.5 87.1 %all-gather.16.cloned.1.call-start = ((), (), s32[]{:S(2)}) async-start(), calls=%async_computation.9 | async-start | bytes 2129920 | tf_op jit(solution)/shard_map/all_gather | solution.py:113
  7.3 172.0 %all-gather.10.cloned.1.call-start = ((), (), s32[]{:S(2)}) async-start(), calls=%async_computation.6 | async-start | bytes 1331200 | tf_op jit(solution)/shard_map/all_gather | solution.py:121
  93.7 2.3 copy-start.9
  95.9 1.7 copy-start.13
  95.9 2.9 copy-start.14
  97.6 3.7 copy-start.26
  180.5 1.3 copy-start.2
  208.4 35.6 %all-to-all-start.2 = ((f32[1,128,32]{2,0,1:T(1,128)}), f32[1,128,32]{2,0,1:T(1,128)S(1)}, u32[]{:S(2)}, u32[]{:S(2)}) async-start(f32[1,128,32]{2,0,1:T(1,128)} %bitcast.73), calls=%async_computation.2 | async-start | bytes 131072 | tf_op jit(solution)/shard_map/all_to_all | solution.py:140
  244.0 9.8 %copy-start.16 = (f32[1,128,32]{2,0,1:T(1,128)}, f32[1,128,32]{2,0,1:T(1,128)S(1)}, u32[]{:S(2)}) copy-start(f32[1,128,32]{2,0,1:T(1,128)S(1)} %all-to-all-done.2) | copy-start | bytes 49156
  244.0 14.3 %all-to-all-start.1 = ((f32[1,128,32]{2,0,1:T(1,128)}), f32[1,128,32]{2,0,1:T(1,128)S(1)}, u32[]{:S(2)}, u32[]{:S(2)}) async-start(f32[1,128,32]{2,0,1:T(1,128)} %bitcast.70), calls=%async_computation.1 | async-start | bytes 131072 | tf_op jit(solution)/shard_map/all_to_all | solution.py:139
  258.3 57.1 %all-to-all-start = ((f32[1,128,4096]{2,0,1:T(1,128)}), f32[1,128,4096]{2,0,1:T(1,128)S(1)}, u32[]{:S(2)}, u32[]{:S(2)}) async-start(f32[1,128,4096]{2,0,1:T(1,128)} %broadcast_in_dim.169), calls=%async_computation | async-start | bytes 4194304 | tf_op jit(solution)/shard_map/all_to_all | solution.py:141
  264.2 136.0 %all-gather.18.cloned.1.call-start = ((), (), s32[]{:S(2)}) async-start(), calls=%async_computation.10 | async-start | bytes 1064960 | tf_op jit(solution)/shard_map/all_gather | solution.py:145
  320.3 81.4 %copy-start.7 = (bf16[1,4096,128]{2,1,0:T(8,128)(2,1)S(1)}, bf16[1,4096,128]{2,1,0:T(8,128)(2,1)}, u32[]{:S(2)}) copy-start(bf16[1,4096,128]{2,1,0:T(8,128)(2,1)} %param.28) | copy-start | bytes 3145732
  320.3 81.4 %copy-start.21 = (bf16[1,128,128]{2,1,0:T(8,128)(2,1)S(1)}, bf16[1,128,128]{2,1,0:T(8,128)(2,1)}, u32[]{:S(2)}) copy-start(bf16[1,128,128]{2,1,0:T(8,128)(2,1)} %param.22) | copy-start | bytes 98308
  321.0 85.5 %copy-start.25 = (bf16[1,128,128]{2,1,0:T(8,128)(2,1)S(1)}, bf16[1,128,128]{2,1,0:T(8,128)(2,1)}, u32[]{:S(2)}) copy-start(bf16[1,128,128]{2,1,0:T(8,128)(2,1)} %param.23) | copy-start | bytes 98308
  321.0 164.5 %all-gather.12.cloned.1.call-start = ((), (), s32[]{:S(2)}) async-start(), calls=%async_computation.7 | async-start | bytes 2129920 | tf_op jit(solution)/shard_map/all_gather | solution.py:113
  401.7 86.0 %copy-start.28 = (f32[1,8192]{1,0:T(1,128)S(1)}, f32[1,8192]{1,0:T(1,128)}, u32[]{:S(2)}) copy-start(f32[1,8192]{1,0:T(1,128)} %param.26) | copy-start | bytes 98308
  402.2 87.2 %copy-start.22 = (bf16[128,128]{1,0:T(8,128)(2,1)}, bf16[128,128]{1,0:T(8,128)(2,1)S(1)}, u32[]{:S(2)}) copy-start(bf16[128,128]{1,0:T(8,128)(2,1)S(1)} %fusion.91) | copy-start | bytes 98308
  402.2 4.3 collective-permute-start
  407.1 163.9 %all-gather.14.cloned.1.call-start = ((), (), s32[]{:S(2)}) async-start(), calls=%async_computation.8 | async-start | bytes 1331200 | tf_op jit(solution)/shard_map/all_gather | solution.py:121
  485.5 2.3 copy-start.10
  572.3 1.6 copy-start.24
  592.5 34.1 %all-to-all-start.5 = ((f32[1,128,32]{2,0,1:T(1,128)}), f32[1,128,32]{2,0,1:T(1,128)S(1)}, u32[]{:S(2)}, u32[]{:S(2)}) async-start(f32[1,128,32]{2,0,1:T(1,128)} %bitcast.95), calls=%async_computation.5 | async-start | bytes 131072 | tf_op jit(solution)/shard_map/all_to_all | solution.py:140
  626.6 14.3 %all-to-all-start.4 = ((f32[1,128,32]{2,0,1:T(1,128)}), f32[1,128,32]{2,0,1:T(1,128)S(1)}, u32[]{:S(2)}, u32[]{:S(2)}) async-start(f32[1,128,32]{2,0,1:T(1,128)} %bitcast.92), calls=%async_computation.4 | async-start | bytes 131072 | tf_op jit(solution)/shard_map/all_to_all | solution.py:139
  640.9 57.1 %all-to-all-start.3 = ((f32[1,128,4096]{2,0,1:T(1,128)}), f32[1,128,4096]{2,0,1:T(1,128)S(1)}, u32[]{:S(2)}, u32[]{:S(2)}) async-start(f32[1,128,4096]{2,0,1:T(1,128)} %broadcast_in_dim.172), calls=%async_computation.3 | async-start | bytes 4194304 | tf_op jit(solution)/shard_map/all_to_all | solution.py:141
  646.8 136.1 %all-gather.20.cloned.1.call-start = ((), (), s32[]{:S(2)}) async-start(), calls=%async_computation.11 | async-start | bytes 1064960 | tf_op jit(solution)/shard_map/all_gather | solution.py:145
  702.9 81.5 %copy-start.8 = (bf16[1,4096,128]{2,1,0:T(8,128)(2,1)S(1)}, bf16[1,4096,128]{2,1,0:T(8,128)(2,1)}, u32[]{:S(2)}) copy-start(bf16[1,4096,128]{2,1,0:T(8,128)(2,1)} %param.28) | copy-start | bytes 3145732
  702.9 81.5 %copy-start.15 = (bf16[128,128]{1,0:T(8,128)(2,1)S(1)}, bf16[128,128]{1,0:T(8,128)(2,1)}, u32[]{:S(2)}) copy-start(bf16[128,128]{1,0:T(8,128)(2,1)} %bitcast_select_fusion) | copy-start | bytes 98308
  703.6 81.2 %copy-start.23 = (bf16[128,128]{1,0:T(8,128)(2,1)S(1)}, bf16[128,128]{1,0:T(8,128)(2,1)}, u32[]{:S(2)}) copy-start(bf16[128,128]{1,0:T(8,128)(2,1)} %copy-done.22) | copy-start | bytes 98308
  703.6 81.8 %copy-start.1 = (bf16[1,8192,80]{1,2,0:T(8,128)(2,1)S(1)}, bf16[1,8192,80]{1,2,0:T(8,128)(2,1)}, u32[]{:S(2)}) copy-start(bf16[1,8192,80]{1,2,0:T(8,128)(2,1)} %param.27) | copy-start | bytes 3932164
Sparse Core Ops, SparseCore 0:
  10.5 83.1 all-gather.15
  97.7 81.4 all-gather.9
  321.1 79.0 all-gather.17
  407.2 78.1 all-gather.11
  489.5 81.4 all-gather.13
  703.7 79.1 all-gather.19
where the time goes:
time: 800 us; the launch traced here: 793 us
  waiting for transfers between devices  610 us (76%)
  starting transfers between devices  74.2 us (9%)
  local copies, waits for them, and re-layouts  35 us (4%)
  matrix products  26.5 us (3%)
  other arithmetic  22.1 us (3%)
  between operations  16.8 us (2%)
  loops' own time  8.38 us (1%)
    all_gather x2, waiting for transfers between devices, on_device(): gathered = lax.all_gather(current, 'kv', axis=1, tiled=True)  164 us
    all_gather x2, waiting for transfers between devices, on_device(): lax.all_gather(attended, 'kv', axis=0, tiled=True)  158 us
    all_gather x2, waiting for transfers between devices, on_device(): united = lax.all_gather(local_cols, 'kv', axis=1, tiled=True)  157 us
    all_to_all x2, waiting for transfers between devices, on_device(): lax.all_to_all(partial_value[2][None], 'kv', split_axis=1, concat_axis=0,...  100 us
    all_to_all x2, starting transfers between devices, on_device(): lax.all_to_all(partial_value[1][None], 'kv', split_axis=1, concat_axis=0,...  49.9 us
    all_to_all x2, waiting for transfers between devices, on_device(): lax.all_to_all(partial_value[1][None], 'kv', split_axis=1, concat_axis=0,...  18.3 us
  transfers between devices with their start and end apart: 13, of which 13 were waited for; matrix products, arithmetic and copies ran while one was open for 2% of the time, Pallas kernels for 0%

commit v1 on v0

--- a/solution.py
+++ b/solution.py
@@ -118,7 +118,9 @@
         local_cols = jnp.dot(normed, weight_in, preferred_element_type=jnp.float32).astype(
             jnp.bfloat16
         )
-        united = lax.all_gather(local_cols, "kv", axis=1, tiled=True)
+        united = jnp.concatenate(
+            lax.all_to_all(jnp.stack([local_cols] * lax.axis_size("kv")), "kv", 0, 0), axis=1
+        )
         query = united[:, : HEADS_Q * HD].reshape(row_count, HEADS_Q, HD)
         new_keys = united[:, HEADS_Q * HD : (HEADS_Q + KV_HEADS) * HD].reshape(
             row_count, KV_HEADS, HD

time: 800 us -> 717 us (0.90)
  waiting for transfers between devices: 610 us -> 480 us
  blocking collectives: 0 us -> 42.2 us
    all_gather x2 -> x0, waiting for transfers between devices: 157 us -> none  [on_device(): united = lax.all_gather(local_cols, 'kv', axis=1, tiled=True)]
    all_to_all x0 -> x1, blocking collectives: none -> 42.2 us  [on_device(): lax.all_to_all(jnp.stack([local_cols] * lax.axis_size('kv')), 'kv', 0, 0)]
    all_to_all x0 -> x1, waiting for transfers between devices: none -> 26.9 us  [on_device(): lax.all_to_all(jnp.stack([local_cols] * lax.axis_size('kv')), 'kv', 0, 0)]
    all_to_all x0 -> x1, starting transfers between devices: none -> 8.07 us  [on_device(): lax.all_to_all(jnp.stack([local_cols] * lax.axis_size('kv')), 'kv', 0, 0)]
  transfers between devices with their start and end apart: 13 -> 12, of which waited for: 13 -> 12; matrix products, arithmetic and copies ran while one was open for 2% -> 3% of each run, Pallas kernels for 0% -> 0%
where the time goes in v1:
time: 717 us; the launch traced here: 709 us
  waiting for transfers between devices  480 us (67%)
  starting transfers between devices  79.9 us (11%)
  blocking collectives  42.2 us (6%)
  local copies, waits for them, and re-layouts  34.4 us (5%)
  matrix products  25.2 us (4%)
  other arithmetic  22.1 us (3%)
  between operations  16.5 us (2%)
  loops' own time  9.29 us (1%)
    all_gather x2, waiting for transfers between devices, on_device(): gathered = lax.all_gather(current, 'kv', axis=1, tiled=True)  165 us
    all_gather x2, waiting for transfers between devices, on_device(): lax.all_gather(attended, 'kv', axis=0, tiled=True)  158 us
    all_to_all x2, waiting for transfers between devices, on_device(): lax.all_to_all(partial_value[2][None], 'kv', split_axis=1, concat_axis=0,...  100 us
    all_to_all x2, starting transfers between devices, on_device(): lax.all_to_all(partial_value[1][None], 'kv', split_axis=1, concat_axis=0,...  47.9 us
    all_to_all x1, blocking collectives, on_device(): lax.all_to_all(jnp.stack([local_cols] * lax.axis_size('kv')), 'kv', 0, 0)  42.2 us
    all_to_all x1, waiting for transfers between devices, on_device(): lax.all_to_all(jnp.stack([local_cols] * lax.axis_size('kv')), 'kv', 0, 0)  26.9 us
    all_to_all x2, waiting for transfers between devices, on_device(): lax.all_to_all(partial_value[1][None], 'kv', split_axis=1, concat_axis=0,...  18.3 us
  transfers between devices with their start and end apart: 12, of which 12 were waited for; matrix products, arithmetic and copies ran while one was open for 3% of the time, Pallas kernels for 0%

profile of v1, /device:TPU:1, one launch (start us, length us, event | category | flops | bytes accessed | tf_op | source)
XLA Modules:
  0.0 709.4 jit_solution(13345825434212861684)
XLA Ops:
  7.3 86.4 %all-gather.10.cloned.1.call-done = bf16[1,128,8192]{2,1,0:T(8,128)(2,1)} async-done(((bf16[1,128,128]{2,1,0:T(8,128)(2,1)}), bf16[1,128,8192]{2,1,0:T(8,128)(2,1)}) %all-gather.10.cloned.1.call-update) | async-done | bytes 2097168 | tf_op jit(solution)/shard_map/all_gather | solution.py:113
  93.7 2.2 fusion.77
  98.2 8.1 %all-to-all-start = ((bf16[64,128,80]{1,2,0:T(8,128)(2,1)}), bf16[64,128,80]{1,2,0:T(8,128)(2,1)S(1)}, u32[]{:S(2)}, u32[]{:S(2)}) async-start(bf16[64,128,80]{1,2,0:T(8,128)(2,1)} %stack.10), calls=%async_computation | async-start | bytes 2621440 | tf_op jit(solution)/shard_map/all_to_all | solution.py:122
  113.5 26.9 %all-to-all-done = bf16[64,128,80]{1,2,0:T(8,128)(2,1)S(1)} async-done(((bf16[64,128,80]{1,2,0:T(8,128)(2,1)}), bf16[64,128,80]{1,2,0:T(8,128)(2,1)S(1)}, u32[]{:S(2)}, u32[]{:S(2)}) %all-to-all-start) | async-done | bytes 1310752 | tf_op jit(solution)/shard_map/all_to_all | solution.py:122
  142.1 13.6 %while.58 = (s32[]{:T(128)}, f32[4,128,8]{1,2,0:T(8,128)S(1)}, f32[4,128,8]{1,2,0:T(8,128)S(1)}, f32[4,128,8,128]{3,1,2,0:T(8,128)S(1)}, bf16[4,128,8,128]{1,3,2...) while((s32[]{:T(128)}, f32[4,128,8]{1,2,0:T(8,128)S(1)}, ...), condition=%wide.region_4.5_spmd.clone, body=%wide.region_1.4_spmd.clone.sunk | while | flops 204863488 | bytes 5737833 | solution.py:44
  142.1 1.5 select_reduce_fusion.8
  144.1 1.3 fusion.142
  145.5 1.5 select_reduce_fusion.8
  147.5 1.3 fusion.142
  148.9 1.5 select_reduce_fusion.8
  150.9 1.3 fusion.142
  152.3 1.5 select_reduce_fusion.8
  154.3 1.3 fusion.142
  155.7 13.0 %conditional.2 = (f32[128,32]{0,1:T(8,128)S(1)}, f32[128,32]{0,1:T(8,128)S(1)}, f32[128,4096]{1,0:T(8,128)}) conditional(s32[]{:T(128)} %convert_element_type.53, (f32[128,4,8,128]{3,0,2,1:T(8,128)S(1)}, f32[128,32]{0,1:T(8,128)S(1)}, f32[128,32]{0,1:T(8,128)S(1)}) %tuple.191, (bf16[128,4096]{0,1:T(8,128)(2,1)}, bf16[128,5120]{0,1:T(8,128)(2,1)}, ...), branch_computations={%region_5.6_spmd, %region_6.11_spmd} | conditional | flops 69883904 | bytes 51759524 | solution.py:139
  156.9 3.0 copy.129
  169.4 24.3 %all-to-all-start.3 = ((f32[1,128,32]{2,0,1:T(1,128)}), f32[1,128,32]{2,0,1:T(1,128)S(1)}, u32[]{:S(2)}, u32[]{:S(2)}) async-start(f32[1,128,32]{2,0,1:T(1,128)} %bitcast.76), calls=%async_computation.3 | async-start | bytes 131072 | tf_op jit(solution)/shard_map/all_to_all | solution.py:142
  194.4 9.2 %all-to-all-done.3 = f32[1,128,32]{2,0,1:T(1,128)S(1)} async-done(((f32[1,128,32]{2,0,1:T(1,128)}), f32[1,128,32]{2,0,1:T(1,128)S(1)}, u32[]{:S(2)}, u32[]{:S(2)}) %all-to-all-start.3) | async-done | bytes 16416 | tf_op jit(solution)/shard_map/all_to_all | solution.py:142
  203.5 4.4 all-to-all-start.2
  207.9 5.3 broadcast_in_dim.169
  213.2 4.6 all-to-all-done.2
  217.8 5.9 all-to-all-start.1
  225.4 49.5 %all-to-all-done.1 = f32[1,128,4096]{2,0,1:T(1,128)S(1)} async-done(((f32[1,128,4096]{2,0,1:T(1,128)}), f32[1,128,4096]{2,0,1:T(1,128)S(1)}, u32[]{:S(2)}, u32[]{:S(2)}) %all-to-all-start.1) | async-done | bytes 2097184 | tf_op jit(solution)/shard_map/all_to_all | solution.py:143
  275.5 4.3 multiply_reduce_fusion.1
  280.5 79.2 %all-gather.12.cloned.1.call-done = bf16[64,2,4096]{2,1,0:T(2,128)(2,1)} async-done(((bf16[1,2,4096]{2,1,0:T(2,128)(2,1)}), bf16[64,2,4096]{2,1,0:T(2,128)(2,1)}) %all-gather.12.cloned.1.call-update) | async-done | bytes 1048592 | tf_op jit(solution)/shard_map/all_gather | solution.py:147
  359.7 1.5 reshape.210
  361.7 3.3 collective-permute-start
  366.6 78.3 %all-gather.8.cloned.1.call-done = bf16[128,8192]{1,0:T(8,128)(2,1)} async-done(((bf16[128,128]{1,0:T(8,128)(2,1)}), bf16[128,8192]{1,0:T(8,128)(2,1)}) %all-gather.8.cloned.1.call-update) | async-done | bytes 2097168 | tf_op jit(solution)/shard_map/all_gather | solution.py:113
  445.0 2.2 fusion.74
  448.4 42.2 %all_to_all.82 = bf16[64,128,80]{1,2,0:T(8,128)(2,1)S(1)} all-to-all(bf16[64,128,80]{1,2,0:T(8,128)(2,1)S(1)} %stack.12), channel_id=1, replica_groups=mesh['section'=8,'kv'=64] {'kv'}, dimensions={0} | all-to-all | bytes 2621440 | tf_op jit(solution)/shard_map/all_to_all | solution.py:122
  491.7 13.3 %while.59 = (s32[]{:T(128)}, f32[4,128,8]{1,2,0:T(8,128)S(1)}, f32[4,128,8]{1,2,0:T(8,128)S(1)}, f32[4,128,8,128]{3,1,2,0:T(8,128)S(1)}, bf16[4,128,8,128]{1,3,2...) while((s32[]{:T(128)}, f32[4,128,8]{1,2,0:T(8,128)S(1)}, ...), condition=%wide.region_18.19_spmd.clone, body=%wide.region_15.18_spmd.clone.sunk | while | flops 204863488 | bytes 5737961 | solution.py:44
  491.7 1.4 select_reduce_fusion.9
  493.7 1.3 fusion.146
  495.1 1.4 select_reduce_fusion.9
  497.0 1.3 fusion.146
  498.4 1.4 select_reduce_fusion.9
  501.7 1.4 select_reduce_fusion.9
  505.0 4.4 conditional.3
  506.2 3.0 copy.130
  510.1 23.7 %all-to-all-start.7 = ((f32[1,128,32]{2,0,1:T(1,128)}), f32[1,128,32]{2,0,1:T(1,128)S(1)}, u32[]{:S(2)}, u32[]{:S(2)}) async-start(f32[1,128,32]{2,0,1:T(1,128)} %bitcast.101), calls=%async_computation.7 | async-start | bytes 131072 | tf_op jit(solution)/shard_map/all_to_all | solution.py:142
  534.5 9.2 %all-to-all-done.7 = f32[1,128,32]{2,0,1:T(1,128)S(1)} async-done(((f32[1,128,32]{2,0,1:T(1,128)}), f32[1,128,32]{2,0,1:T(1,128)S(1)}, u32[]{:S(2)}, u32[]{:S(2)}) %all-to-all-start.7) | async-done | bytes 16416 | tf_op jit(solution)/shard_map/all_to_all | solution.py:142
  543.7 4.4 all-to-all-start.6
  548.1 5.3 broadcast_in_dim.172
  553.4 4.6 all-to-all-done.6
  558.0 5.9 all-to-all-start.5
  564.1 50.9 %all-to-all-done.5 = f32[1,128,4096]{2,0,1:T(1,128)S(1)} async-done(((f32[1,128,4096]{2,0,1:T(1,128)}), f32[1,128,4096]{2,0,1:T(1,128)S(1)}, u32[]{:S(2)}, u32[]{:S(2)}) %all-to-all-start.5) | async-done | bytes 2097184 | tf_op jit(solution)/shard_map/all_to_all | solution.py:143
  615.6 4.3 multiply_reduce_fusion
  620.6 79.3 %all-gather.14.cloned.1.call-done = bf16[64,2,4096]{2,1,0:T(2,128)(2,1)} async-done(((bf16[1,2,4096]{2,1,0:T(2,128)(2,1)}), bf16[64,2,4096]{2,1,0:T(2,128)(2,1)}) %all-gather.14.cloned.1.call-update) | async-done | bytes 1048592 | tf_op jit(solution)/shard_map/all_gather | solution.py:147
  699.9 1.5 reshape.212
  (106 shorter events, 31.5 us)
Async XLA Ops:
  6.5 89.4 %copy-start = (bf16[1,8192,80]{1,2,0:T(8,128)(2,1)S(1)}, bf16[1,8192,80]{1,2,0:T(8,128)(2,1)}, u32[]{:S(2)}) copy-start(bf16[1,8192,80]{1,2,0:T(8,128)(2,1)} %param.27) | copy-start | bytes 3932164
  6.5 89.4 %copy-start.27 = (f32[1,8192]{1,0:T(1,128)S(1)}, f32[1,8192]{1,0:T(1,128)}, u32[]{:S(2)}) copy-start(f32[1,8192]{1,0:T(1,128)} %param.26) | copy-start | bytes 98308
  6.5 87.1 %all-gather.10.cloned.1.call-start = ((), (), s32[]{:S(2)}) async-start(), calls=%async_computation.9 | async-start | bytes 2129920 | tf_op jit(solution)/shard_map/all_gather | solution.py:113
  93.7 2.3 copy-start.10
  97.0 9.4 %copy-start.14 = (bf16[1,384,512]{2,1,0:T(8,128)(2,1)S(1)}, bf16[1,384,512]{2,1,0:T(8,128)(2,1)}, u32[]{:S(2)}) copy-start(bf16[1,384,512]{2,1,0:T(8,128)(2,1)} %param.29) | copy-start | bytes 1179652
  98.2 42.2 %all-to-all-start = ((bf16[64,128,80]{1,2,0:T(8,128)(2,1)}), bf16[64,128,80]{1,2,0:T(8,128)(2,1)S(1)}, u32[]{:S(2)}, u32[]{:S(2)}) async-start(bf16[64,128,80]{1,2,0:T(8,128)(2,1)} %stack.10), calls=%async_computation | async-start | bytes 2621440 | tf_op jit(solution)/shard_map/all_to_all | solution.py:122
  106.3 4.6 copy-start.26
  140.4 1.4 copy-start.6
  169.4 34.2 %all-to-all-start.3 = ((f32[1,128,32]{2,0,1:T(1,128)}), f32[1,128,32]{2,0,1:T(1,128)S(1)}, u32[]{:S(2)}, u32[]{:S(2)}) async-start(f32[1,128,32]{2,0,1:T(1,128)} %bitcast.76), calls=%async_computation.3 | async-start | bytes 131072 | tf_op jit(solution)/shard_map/all_to_all | solution.py:142
  203.5 9.7 %copy-start.16 = (f32[1,128,32]{2,0,1:T(1,128)}, f32[1,128,32]{2,0,1:T(1,128)S(1)}, u32[]{:S(2)}) copy-start(f32[1,128,32]{2,0,1:T(1,128)S(1)} %all-to-all-done.3) | copy-start | bytes 49156
  203.5 14.3 %all-to-all-start.2 = ((f32[1,128,32]{2,0,1:T(1,128)}), f32[1,128,32]{2,0,1:T(1,128)S(1)}, u32[]{:S(2)}, u32[]{:S(2)}) async-start(f32[1,128,32]{2,0,1:T(1,128)} %bitcast.73), calls=%async_computation.2 | async-start | bytes 131072 | tf_op jit(solution)/shard_map/all_to_all | solution.py:141
  217.8 57.1 %all-to-all-start.1 = ((f32[1,128,4096]{2,0,1:T(1,128)}), f32[1,128,4096]{2,0,1:T(1,128)S(1)}, u32[]{:S(2)}, u32[]{:S(2)}) async-start(f32[1,128,4096]{2,0,1:T(1,128)} %broadcast_in_dim.169), calls=%async_computation.1 | async-start | bytes 4194304 | tf_op jit(solution)/shard_map/all_to_all | solution.py:143
  223.7 136.1 %all-gather.12.cloned.1.call-start = ((), (), s32[]{:S(2)}) async-start(), calls=%async_computation.10 | async-start | bytes 1064960 | tf_op jit(solution)/shard_map/all_gather | solution.py:147
  279.8 81.4 %copy-start.8 = (bf16[1,4096,128]{2,1,0:T(8,128)(2,1)S(1)}, bf16[1,4096,128]{2,1,0:T(8,128)(2,1)}, u32[]{:S(2)}) copy-start(bf16[1,4096,128]{2,1,0:T(8,128)(2,1)} %param.28) | copy-start | bytes 3145732
  279.8 81.4 %copy-start.21 = (bf16[1,128,128]{2,1,0:T(8,128)(2,1)S(1)}, bf16[1,128,128]{2,1,0:T(8,128)(2,1)}, u32[]{:S(2)}) copy-start(bf16[1,128,128]{2,1,0:T(8,128)(2,1)} %param.22) | copy-start | bytes 98308
  280.5 85.5 %copy-start.25 = (bf16[1,128,128]{2,1,0:T(8,128)(2,1)S(1)}, bf16[1,128,128]{2,1,0:T(8,128)(2,1)}, u32[]{:S(2)}) copy-start(bf16[1,128,128]{2,1,0:T(8,128)(2,1)} %param.23) | copy-start | bytes 98308
  280.5 164.5 %all-gather.8.cloned.1.call-start = ((), (), s32[]{:S(2)}) async-start(), calls=%async_computation.8 | async-start | bytes 2129920 | tf_op jit(solution)/shard_map/all_gather | solution.py:113
  361.2 86.0 %copy-start.28 = (f32[1,8192]{1,0:T(1,128)S(1)}, f32[1,8192]{1,0:T(1,128)}, u32[]{:S(2)}) copy-start(f32[1,8192]{1,0:T(1,128)} %param.26) | copy-start | bytes 98308
  361.7 86.6 %copy-start.22 = (bf16[128,128]{1,0:T(8,128)(2,1)}, bf16[128,128]{1,0:T(8,128)(2,1)S(1)}, u32[]{:S(2)}) copy-start(bf16[128,128]{1,0:T(8,128)(2,1)S(1)} %fusion.91) | copy-start | bytes 98308
  361.7 4.3 collective-permute-start
  445.0 2.3 copy-start.11
  490.6 1.1 copy-start.7
  490.6 1.1 copy-start.24
  510.1 33.6 %all-to-all-start.7 = ((f32[1,128,32]{2,0,1:T(1,128)}), f32[1,128,32]{2,0,1:T(1,128)S(1)}, u32[]{:S(2)}, u32[]{:S(2)}) async-start(f32[1,128,32]{2,0,1:T(1,128)} %bitcast.101), calls=%async_computation.7 | async-start | bytes 131072 | tf_op jit(solution)/shard_map/all_to_all | solution.py:142
  543.7 14.3 %all-to-all-start.6 = ((f32[1,128,32]{2,0,1:T(1,128)}), f32[1,128,32]{2,0,1:T(1,128)S(1)}, u32[]{:S(2)}, u32[]{:S(2)}) async-start(f32[1,128,32]{2,0,1:T(1,128)} %bitcast.98), calls=%async_computation.6 | async-start | bytes 131072 | tf_op jit(solution)/shard_map/all_to_all | solution.py:141
  558.0 57.1 %all-to-all-start.5 = ((f32[1,128,4096]{2,0,1:T(1,128)}), f32[1,128,4096]{2,0,1:T(1,128)S(1)}, u32[]{:S(2)}, u32[]{:S(2)}) async-start(f32[1,128,4096]{2,0,1:T(1,128)} %broadcast_in_dim.172), calls=%async_computation.5 | async-start | bytes 4194304 | tf_op jit(solution)/shard_map/all_to_all | solution.py:143
  563.8 136.1 %all-gather.14.cloned.1.call-start = ((), (), s32[]{:S(2)}) async-start(), calls=%async_computation.11 | async-start | bytes 1064960 | tf_op jit(solution)/shard_map/all_gather | solution.py:147
  619.9 81.4 %copy-start.9 = (bf16[1,4096,128]{2,1,0:T(8,128)(2,1)S(1)}, bf16[1,4096,128]{2,1,0:T(8,128)(2,1)}, u32[]{:S(2)}) copy-start(bf16[1,4096,128]{2,1,0:T(8,128)(2,1)} %param.28) | copy-start | bytes 3145732
  619.9 81.4 %copy-start.15 = (bf16[128,128]{1,0:T(8,128)(2,1)S(1)}, bf16[128,128]{1,0:T(8,128)(2,1)}, u32[]{:S(2)}) copy-start(bf16[128,128]{1,0:T(8,128)(2,1)} %bitcast_select_fusion) | copy-start | bytes 98308
  620.6 81.2 %copy-start.23 = (bf16[128,128]{1,0:T(8,128)(2,1)S(1)}, bf16[128,128]{1,0:T(8,128)(2,1)}, u32[]{:S(2)}) copy-start(bf16[128,128]{1,0:T(8,128)(2,1)} %copy-done.22) | copy-start | bytes 98308
  620.6 81.8 %copy-start.1 = (bf16[1,8192,80]{1,2,0:T(8,128)(2,1)S(1)}, bf16[1,8192,80]{1,2,0:T(8,128)(2,1)}, u32[]{:S(2)}) copy-start(bf16[1,8192,80]{1,2,0:T(8,128)(2,1)} %param.27) | copy-start | bytes 3932164
Sparse Core Ops, SparseCore 0:
  10.5 83.1 all-gather.9
  280.6 79.1 all-gather.11
  366.7 78.1 all-gather.7
  620.7 79.1 all-gather.13
